TPU v7x, 512 devices: a whole 4x4x16 slice. The times are simulated.
512 devices in a mesh: tm: 128 (over z, y, core), chan: 4 (over x).
Axes of the slice: x: 4, y: 4, z: 16, core: 2. Of those that a mesh axis runs over, the one named last changes fastest.
Arguments:
- series: bfloat16 [32768, 512], P('tm', 'chan'), may hold values from -6 to 6
- proj_weight: bfloat16 [512, 3, 512], P(None, None, 'chan'), may hold values from -0.25 to 0.25
- proj_bias: float32 [3, 512], P(None, 'chan'), may hold values from -6 to 6
- short_taps: float32 [3, 3, 512], P(None, None, 'chan'), may hold values from -6 to 6
- short_bias: float32 [3, 512], P(None, 'chan'), may hold values from -6 to 6
- spectrum: float32 [2, 128, 2, 256, 512], P(None, 'tm', None, None, 'chan'), may hold values from -6 to 6
- skip_gain: float32 [512], P('chan'), may hold values from -6 to 6
- out_weight: bfloat16 [512, 512], replicated, may hold values from -0.25 to 0.25
- out_bias: float32 [512], P('chan'), may hold values from -6 to 6
Outputs:
- mixed_out: bfloat16 [32768, 512], P('tm', 'chan')
All inputs are finite; a program needn't handle non-finite values.
Results may differ from a plain program's by a relative error of at most 0.009.
Values may be sent and summed in bfloat16 or wider, within the bound.
No kernel may reach another device: no remote copies, remote signals or barrier semaphores. Data moves between devices by JAX's collectives and lax.ppermute only.
A program may use at most 64 MiB of HBM per device.

v0:
```python
import math
import jax
import jax.numpy as jnp
import numpy as np
from jax import lax
from jax.sharding import PartitionSpec as P

HI = lax.Precision.HIGHEST


def from_behind(array, axis, by):
    length = lax.axis_size(axis)
    pairs = [(i, i + by) for i in range(length) if 0 <= i + by < length]
    return lax.ppermute(array, axis, pairs)


def reverse_bits_np(values, digits):
    result = np.zeros_like(values)
    for bit_level in range(digits):
        result = result | (values >> bit_level & 1) << digits - 1 - bit_level
    return result


def dft_tables(tm_count, steps_dev):
    rows = 2 * tm_count
    digits = tm_count.bit_length() - 1
    r = np.arange(rows)
    k1 = 2 * reverse_bits_np(r // 2, digits) + r % 2
    m = np.arange(tm_count)
    t = np.arange(steps_dev)
    b = np.arange(steps_dev)
    period = rows * steps_dev
    ang1 = 2 * np.pi * (k1[:, None] * m[None, :] % rows) / rows
    ang2 = 2 * np.pi * (t[:, None] * b[None, :] % steps_dev) / steps_dev
    angt = 2 * np.pi * (k1[:, None] * t[None, :] % period) / period
    f32 = lambda a: jnp.asarray(a.astype(np.float32))
    return dict(
        c1=f32(np.cos(ang1)),
        s1=f32(np.sin(ang1)),
        c2=f32(np.cos(ang2)),
        s2=f32(np.sin(ang2)),
        ct=f32(np.cos(angt)),
        st=f32(np.sin(angt)),
        period=period,
    )


def mm(a, b):
    return jnp.dot(a, b, precision=HI, preferred_element_type=jnp.float32)


def long_conv(x, h, tab):
    c1, s1, c2, s2, ct, st = (tab[k] for k in ("c1", "s1", "c2", "s2", "ct", "st"))
    ar = mm(c1, x)
    ai = -mm(s1, x)
    tr = ar * ct + ai * st
    ti = ai * ct - ar * st
    zr = mm(tr, c2) + mm(ti, s2)
    zi = mm(ti, c2) - mm(tr, s2)
    yr = h[0] * zr - h[1] * zi
    yi = h[0] * zi + h[1] * zr
    br = mm(yr, c2) - mm(yi, s2)
    bi = mm(yi, c2) + mm(yr, s2)
    ur = br * ct - bi * st
    ui = bi * ct + br * st
    y = lax.dot_general(
        c1, ur, (((0,), (0,)), ((), ())), precision=HI, preferred_element_type=jnp.float32
    )
    y = y - lax.dot_general(
        s1, ui, (((0,), (0,)), ((), ())), precision=HI, preferred_element_type=jnp.float32
    )
    return y * (1.0 / tab["period"])


def shards(
    series,
    proj_weight,
    proj_bias,
    short_taps,
    short_bias,
    spectrum,
    skip_gain,
    out_weight,
    out_bias,
):
    steps_dev = series.shape[0]
    model_width = proj_weight.shape[0]
    channels = proj_weight.shape[2]
    tm_count = lax.axis_size("tm")
    tab = dft_tables(tm_count, steps_dev)
    flat_weight = proj_weight.reshape(model_width, 3 * channels)
    projected = jnp.dot(
        lax.all_gather(series, "chan", axis=1, tiled=True),
        flat_weight,
        preferred_element_type=jnp.float32,
    )
    projected = (projected.reshape(steps_dev, 3, channels) + proj_bias).astype(jnp.bfloat16)
    taps_count = short_taps.shape[0]
    earlier = from_behind(projected[steps_dev - taps_count + 1 :], "tm", 1)
    extended = jnp.concatenate([earlier, projected], 0).astype(jnp.float32)
    streams = short_bias + short_taps[0] * extended[taps_count - 1 :]
    for offset in range(1, taps_count):
        streams = (
            streams
            + short_taps[offset]
            * extended[taps_count - 1 - offset : taps_count - 1 - offset + steps_dev]
        )
    streams = streams.astype(jnp.bfloat16)
    gate_out = streams[:, 0]
    mixed_in = (streams[:, 1].astype(jnp.float32) * streams[:, 2].astype(jnp.float32)).astype(
        jnp.bfloat16
    )
    pair = jnp.stack([mixed_in, gate_out])[:, None]
    pair = lax.all_to_all(pair, "tm", 3, 1, tiled=True)
    signal_bf = pair[0, :, :, 0]
    gate_own = pair[1, :, :, 0].astype(jnp.float32)
    h = lax.all_to_all(spectrum, "tm", 4, 1, tiled=True)
    h = h.reshape(2, 2 * tm_count, steps_dev)
    signal = signal_bf.astype(jnp.float32)
    convolved = long_conv(signal, h, tab)
    skip = lax.dynamic_index_in_dim(skip_gain, lax.axis_index("tm"), 0, keepdims=False)
    gated = ((convolved + skip * signal) * gate_own).astype(jnp.bfloat16)
    gated = lax.all_to_all(gated[:, :, None], "tm", 0, 2, tiled=True)
    gated = lax.all_gather(gated[0], "chan", axis=1, tiled=True)
    column_start = lax.axis_index("chan") * channels
    weight_cols = lax.dynamic_slice_in_dim(out_weight, column_start, channels, 1)
    mixed_out = jnp.dot(gated, weight_cols, preferred_element_type=jnp.float32) + out_bias
    return mixed_out.astype(jnp.bfloat16)


def solution(mesh):
    return jax.shard_map(
        shards,
        mesh=mesh,
        in_specs=(
            P("tm", "chan"),
            P(None, None, "chan"),
            P(None, "chan"),
            P(None, None, "chan"),
            P(None, "chan"),
            P(None, "tm", None, None, "chan"),
            P("chan"),
            P(),
            P("chan"),
        ),
        out_specs=P("tm", "chan"),
        check_vma=False,
    )
```

profile of v0, /device:TPU:2, one launch (start us, length us, event | category | flops | bytes accessed | tf_op | source)
XLA Modules:
  0.0 140.7 jit_solution(8496077110473266639)
XLA Ops:
  0.0 1.2 copy.32
  1.3 15.2 %all_gather.6 = bf16[256,512]{1,0:T(8,128)(2,1)S(1)} all-gather(bf16[256,128]{1,0:T(8,128)(2,1)S(1)} %copy-done.13), channel_id=1, replica_groups=mesh['tm'=128,'chan'=4] {'chan'}, dimensions={1}, use_global_device_ids=true | all-gather | bytes 327680 | tf_op jit(solution)/shard_map/all_gather | solution.py:93
  16.4 0.3 fusion
  16.8 1.3 collective-permute-start
  18.1 0.8 collective-permute-done
  18.9 0.7 copy-done.16
  19.6 0.1 fusion.9
  19.8 0.8 copy.33
  20.6 20.5 %all-to-all-start.1 = ((bf16[2,1,256,128]{2,0,1,3:T(2,128)(2,1)}), bf16[2,1,256,128]{2,0,1,3:T(2,128)(2,1)S(1)}, u32[]{:S(2)}, u32[]{:S(2)}) async-start(bf16[2,1,256,128]{2,0,1,3:T(2,128)(2,1)} %copy.33), calls=%async_computation.1 | async-start | bytes 262144 | tf_op jit(solution)/shard_map/all_to_all | solution.py:114
  41.1 1.0 copy.31
  42.1 14.4 %all-to-all-done.1 = bf16[2,1,256,128]{2,0,1,3:T(2,128)(2,1)S(1)} async-done(((bf16[2,1,256,128]{2,0,1,3:T(2,128)(2,1)}), bf16[2,1,256,128]{2,0,1,3:T(2,128)(2,1)S(1)}, u32[]{:S(2)}, u32[]{:S(2)}) %all-to-all-start.1) | async-done | bytes 131104 | tf_op jit(solution)/shard_map/all_to_all | solution.py:114
  56.5 7.8 %all-to-all-start = ((f32[2,1,2,256,128]{3,2,1,0,4:T(2,128)}), f32[2,1,2,256,128]{3,2,1,0,4:T(2,128)S(1)}, u32[]{:S(2)}, u32[]{:S(2)}) async-start(f32[2,1,2,256,128]{3,2,1,0,4:T(2,128)} %copy.31), calls=%async_computation | async-start | bytes 1048576 | tf_op jit(solution)/shard_map/all_to_all | solution.py:117
  64.4 0.6 copy-done.18
  65.0 0.6 dynamic_slice.7
  65.6 0.1 copy.34
  65.7 0.8 copy-done.11
  66.5 0.3 convolution_negate_fusion
  66.8 0.3 fusion.26
  67.1 0.4 copy-done.3
  67.5 0.1 copy-done.6
  67.5 0.2 copy-done.2
  67.8 0.4 fusion.23
  68.2 0.6 copy-done.1
  68.7 0.1 copy-done.5
  68.8 1.1 fusion.24
  69.9 0.4 convolution_add_fusion.2
  70.3 24.9 %all-to-all-done = f32[2,1,2,256,128]{3,2,1,0,4:T(2,128)S(1)} async-done(((f32[2,1,2,256,128]{3,2,1,0,4:T(2,128)}), f32[2,1,2,256,128]{3,2,1,0,4:T(2,128)S(1)}, u32[]{:S(2)}, u32[]{:S(2)}) %all-to-all-start) | async-done | bytes 524320 | tf_op jit(solution)/shard_map/all_to_all | solution.py:117
  95.2 0.2 fusion.28
  95.4 0.2 squeeze.23
  95.6 0.2 squeeze.21
  95.8 0.8 copy-done.7
  96.6 1.4 multiply_subtract_fusion
  97.9 0.4 fusion.30
  98.3 0.4 fusion.29
  98.7 0.4 convolution_add_fusion.1
  99.1 0.4 convolution_subtract_fusion
  99.5 0.5 copy-done.9
  100.0 0.6 fusion.18
  100.6 0.3 copy-done.12
  100.9 1.2 fusion.7
  102.1 0.1 copy.36
  102.3 0.5 broadcast.5
  102.8 1.0 reduce
  103.8 0.7 reshape.55
  104.5 9.0 %all-to-all-start.2 = ((bf16[128,2,128]{2,1,0:T(2,128)(2,1)}), bf16[128,2,128]{2,1,0:T(2,128)(2,1)S(1)}, u32[]{:S(2)}, u32[]{:S(2)}) async-start(bf16[128,2,128]{2,1,0:T(2,128)(2,1)} %reshape.55), calls=%async_computation.2 | async-start | bytes 131072 | tf_op jit(solution)/shard_map/all_to_all | solution.py:123
  113.5 14.5 %all-to-all-done.2 = bf16[128,2,128]{2,1,0:T(2,128)(2,1)S(1)} async-done(((bf16[128,2,128]{2,1,0:T(2,128)(2,1)}), bf16[128,2,128]{2,1,0:T(2,128)(2,1)S(1)}, u32[]{:S(2)}, u32[]{:S(2)}) %all-to-all-start.2) | async-done | bytes 65568 | tf_op jit(solution)/shard_map/all_to_all | solution.py:123
  128.0 11.8 %all-gather = bf16[1,256,512,1]{1,2,3,0:T(8,128)(2,1)S(1)} all-gather(bf16[1,256,128,1]{1,2,3,0:T(8,128)(2,1)S(1)} %bitcast.98), channel_id=2, replica_groups=mesh['tm'=128,'chan'=4] {'chan'}, dimensions={2}, use_global_device_ids=true | all-gather | bytes 327680 | tf_op jit(solution)/shard_map/all_gather | solution.py:124
  139.8 0.9 fusion.6
  (35 shorter events, 0.2 us)
Async XLA Ops:
  0.0 139.8 %copy-start = (bf16[512,512]{1,0:T(8,128)(2,1)S(1)}, bf16[512,512]{1,0:T(8,128)(2,1)}, u32[]{:S(2)}) copy-start(bf16[512,512]{1,0:T(8,128)(2,1)} %param.22) | copy-start | bytes 1572868
  0.0 1.2 copy-start.13
  1.2 15.2 %copy-start.15 = (f32[3,128]{1,0:T(4,128)S(1)}, f32[3,128]{1,0:T(4,128)}, u32[]{:S(2)}) copy-start(f32[3,128]{1,0:T(4,128)} %param.17) | copy-start | bytes 4612
  16.4 1.6 %copy-start.14 = (f32[3,3,128]{2,1,0:T(4,128)S(1)}, f32[3,3,128]{2,1,0:T(4,128)}, u32[]{:S(2)}) copy-start(f32[3,3,128]{2,1,0:T(4,128)} %param.18) | copy-start | bytes 13828
  16.8 2.1 %collective-permute-start = (bf16[2,3,128]{2,0,1:T(2,128)(2,1)S(1)}, bf16[2,3,128]{2,0,1:T(2,128)(2,1)S(1)}, u32[]{:S(2)}, u32[]{:S(2)}) collective-permute-start(bf16[2,3,128]{2,0,1:T(2,128)(2,1)S(1)} %slice.63), channel_id=1, source_target_pairs={{0,4},{4,8},{8,12},{12,16},{16,20},{20,24},{24,28},{28,32},{32,36}... | collective-permute-start | bytes 4616 | tf_op jit(solution)/shard_map/ppermute | solution.py:14
  18.9 0.7 copy-start.16
  19.8 21.4 %copy-start.10 = (f32[2,1,2,256,128]{4,3,2,1,0:T(8,128)S(1)}, f32[2,1,2,256,128]{4,3,2,1,0:T(8,128)}, u32[]{:S(2)}) copy-start(f32[2,1,2,256,128]{4,3,2,1,0:T(8,128)} %param.20) | copy-start | bytes 1572868
  20.6 35.9 %all-to-all-start.1 = ((bf16[2,1,256,128]{2,0,1,3:T(2,128)(2,1)}), bf16[2,1,256,128]{2,0,1,3:T(2,128)(2,1)S(1)}, u32[]{:S(2)}, u32[]{:S(2)}) async-start(bf16[2,1,256,128]{2,0,1,3:T(2,128)(2,1)} %copy.33), calls=%async_computation.1 | async-start | bytes 262144 | tf_op jit(solution)/shard_map/all_to_all | solution.py:114
  56.5 38.7 %all-to-all-start = ((f32[2,1,2,256,128]{3,2,1,0,4:T(2,128)}), f32[2,1,2,256,128]{3,2,1,0,4:T(2,128)S(1)}, u32[]{:S(2)}, u32[]{:S(2)}) async-start(f32[2,1,2,256,128]{3,2,1,0,4:T(2,128)} %copy.31), calls=%async_computation | async-start | bytes 1048576 | tf_op jit(solution)/shard_map/all_to_all | solution.py:117
  64.3 0.7 copy-start.18
  65.6 0.9 copy-start.11
  65.6 1.2 copy-start.8
  66.5 1.0 copy-start.3
  66.5 1.0 copy-start.6
  66.8 1.0 copy-start.2
  67.8 0.9 copy-start.1
  67.8 1.0 copy-start.5
  68.8 1.1 copy-start.4
  95.6 1.0 copy-start.7
  99.1 0.9 copy-start.9
  100.0 0.9 copy-start.12
  104.5 23.5 %all-to-all-start.2 = ((bf16[128,2,128]{2,1,0:T(2,128)(2,1)}), bf16[128,2,128]{2,1,0:T(2,128)(2,1)S(1)}, u32[]{:S(2)}, u32[]{:S(2)}) async-start(bf16[128,2,128]{2,1,0:T(2,128)(2,1)} %reshape.55), calls=%async_computation.2 | async-start | bytes 131072 | tf_op jit(solution)/shard_map/all_to_all | solution.py:123
  128.0 11.8 %copy-start.17 = (f32[128]{0:T(128)S(1)}, f32[128]{0:T(128)}, u32[]{:S(2)}) copy-start(f32[128]{0:T(128)} %param.23) | copy-start | bytes 1540
where the time goes:
time: 141 us
  waiting for transfers between devices  54.5 us (39%)
  starting transfers between devices  38.6 us (27%)
  blocking collectives  26.9 us (19%)
  local copies, waits for them, and re-layouts  10.7 us (8%)
  matrix products  8.38 us (6%)
    all_to_all x1, waiting for transfers between devices, shards(): h = lax.all_to_all(spectrum, 'tm', 4, 1, tiled=True)  24.9 us
    all_to_all x1, starting transfers between devices, shards(): pair = lax.all_to_all(pair, 'tm', 3, 1, tiled=True)  20.5 us
    all_gather x1, blocking collectives, shards(): lax.all_gather(series, 'chan', axis=1, tiled=True)  15.2 us
    all_to_all x1, waiting for transfers between devices, shards(): gated = lax.all_to_all(gated[:, :, None], 'tm', 0, 2, tiled=True)  14.5 us
    all_to_all x1, waiting for transfers between devices, shards(): pair = lax.all_to_all(pair, 'tm', 3, 1, tiled=True)  14.4 us
    all_gather x1, blocking collectives, shards(): gated = lax.all_gather(gated[0], 'chan', axis=1, tiled=True)  11.8 us
    all_to_all x1, starting transfers between devices, shards(): gated = lax.all_to_all(gated[:, :, None], 'tm', 0, 2, tiled=True)  9.02 us
    unnamed x44, local copies, waits for them, and re-layouts  8.47 us
  transfers between devices with their start and end apart: 4, of which 4 were waited for; matrix products, arithmetic and copies ran while one was open for 3% of the time, Pallas kernels for 0%

commit v1 on v0

--- a/solution.py
+++ b/solution.py
@@ -121,7 +121,9 @@
     skip = lax.dynamic_index_in_dim(skip_gain, lax.axis_index("tm"), 0, keepdims=False)
     gated = ((convolved + skip * signal) * gate_own).astype(jnp.bfloat16)
     gated = lax.all_to_all(gated[:, :, None], "tm", 0, 2, tiled=True)
-    gated = lax.all_gather(gated[0], "chan", axis=1, tiled=True)
+    gated = jnp.concatenate(
+        lax.all_to_all(jnp.stack([gated[0]] * lax.axis_size("chan")), "chan", 0, 0), axis=1
+    )
     column_start = lax.axis_index("chan") * channels
     weight_cols = lax.dynamic_slice_in_dim(out_weight, column_start, channels, 1)
     mixed_out = jnp.dot(gated, weight_cols, preferred_element_type=jnp.float32) + out_bias

time: 141 us -> 139 us (0.986)
  the two profiles are of different devices: /device:TPU:2 before, /device:TPU:1 now
where the time goes in v1:
time: 139 us
  waiting for transfers between devices  48.6 us (35%)
  starting transfers between devices  35.3 us (25%)
  blocking collectives  34.2 us (25%)
  local copies, waits for them, and re-layouts  10.8 us (8%)
  matrix products  8.38 us (6%)
    all_to_all x1, waiting for transfers between devices, shards(): h = lax.all_to_all(spectrum, 'tm', 4, 1, tiled=True)  24.7 us
    all_to_all x1, blocking collectives, shards(): gated = lax.all_to_all(gated[:, :, None], 'tm', 0, 2, tiled=True)  23.9 us
    all_to_all x1, starting transfers between devices, shards(): pair = lax.all_to_all(pair, 'tm', 3, 1, tiled=True)  18.2 us
    all_to_all x1, waiting for transfers between devices, shards(): pair = lax.all_to_all(pair, 'tm', 3, 1, tiled=True)  15 us
    all_gather x1, blocking collectives, shards(): lax.all_gather(series, 'chan', axis=1, tiled=True)  10.3 us
    unnamed x44, local copies, waits for them, and re-layouts  7.84 us
    all_to_all x1, starting transfers between devices, shards(): h = lax.all_to_all(spectrum, 'tm', 4, 1, tiled=True)  7.23 us
    ppermute x1, starting transfers between devices, from_behind(): return lax.ppermute(array, axis, pairs)  6.27 us
  transfers between devices with their start and end apart: 4, of which 4 were waited for; matrix products, arithmetic and copies ran while one was open for 3% of the time, Pallas kernels for 0%

profile of v1, /device:TPU:1, one launch (start us, length us, event | category | flops | bytes accessed | tf_op | source)
XLA Modules:
  0.0 138.8 jit_solution(14367658271972884744)
XLA Ops:
  0.0 1.2 copy.33
  1.3 10.3 %all_gather.3 = bf16[256,512]{1,0:T(8,128)(2,1)S(1)} all-gather(bf16[256,128]{1,0:T(8,128)(2,1)S(1)} %copy-done.13), channel_id=1, replica_groups=mesh['tm'=128,'chan'=4] {'chan'}, dimensions={1}, use_global_device_ids=true | all-gather | bytes 327680 | tf_op jit(solution)/shard_map/all_gather | solution.py:93
  11.6 0.3 fusion
  11.9 6.3 %collective-permute-start = (bf16[2,3,128]{2,0,1:T(2,128)(2,1)S(1)}, bf16[2,3,128]{2,0,1:T(2,128)(2,1)S(1)}, u32[]{:S(2)}, u32[]{:S(2)}) collective-permute-start(bf16[2,3,128]{2,0,1:T(2,128)(2,1)S(1)} %slice.63), channel_id=1, source_target_pairs={{0,4},{4,8},{8,12},{12,16},{16,20},{20,24},{24,28},{28,32},{32,36}... | collective-permute-start | bytes 4616 | tf_op jit(solution)/shard_map/ppermute | solution.py:14
  18.2 3.3 %collective-permute-done = bf16[2,3,128]{2,0,1:T(2,128)(2,1)S(1)} collective-permute-done((bf16[2,3,128]{2,0,1:T(2,128)(2,1)S(1)}, bf16[2,3,128]{2,0,1:T(2,128)(2,1)S(1)}, u32[]{:S(2)}, u32[]{:S(2)}) %collective-permute-start) | collective-permute-done | bytes 1568 | tf_op jit(solution)/shard_map/ppermute | solution.py:14
  21.6 0.7 copy-done.16
  22.2 0.1 fusion.9
  22.5 0.8 copy.34
  23.3 18.2 %all-to-all-start.1 = ((bf16[2,1,256,128]{2,0,1,3:T(2,128)(2,1)}), bf16[2,1,256,128]{2,0,1,3:T(2,128)(2,1)S(1)}, u32[]{:S(2)}, u32[]{:S(2)}) async-start(bf16[2,1,256,128]{2,0,1,3:T(2,128)(2,1)} %copy.34), calls=%async_computation.1 | async-start | bytes 262144 | tf_op jit(solution)/shard_map/all_to_all | solution.py:114
  41.5 1.0 copy.32
  42.5 15.0 %all-to-all-done.1 = bf16[2,1,256,128]{2,0,1,3:T(2,128)(2,1)S(1)} async-done(((bf16[2,1,256,128]{2,0,1,3:T(2,128)(2,1)}), bf16[2,1,256,128]{2,0,1,3:T(2,128)(2,1)S(1)}, u32[]{:S(2)}, u32[]{:S(2)}) %all-to-all-start.1) | async-done | bytes 131104 | tf_op jit(solution)/shard_map/all_to_all | solution.py:114
  57.5 7.2 %all-to-all-start = ((f32[2,1,2,256,128]{3,2,1,0,4:T(2,128)}), f32[2,1,2,256,128]{3,2,1,0,4:T(2,128)S(1)}, u32[]{:S(2)}, u32[]{:S(2)}) async-start(f32[2,1,2,256,128]{3,2,1,0,4:T(2,128)} %copy.32), calls=%async_computation | async-start | bytes 1048576 | tf_op jit(solution)/shard_map/all_to_all | solution.py:117
  64.7 0.6 copy-done.18
  65.4 0.6 dynamic_slice.7
  66.0 0.1 copy.35
  66.1 0.8 copy-done.11
  66.9 0.3 convolution_negate_fusion
  67.2 0.3 fusion.25
  67.4 0.4 copy-done.3
  67.8 0.1 copy-done.6
  67.9 0.2 copy-done.2
  68.2 0.4 fusion.22
  68.5 0.5 copy-done.1
  69.1 0.1 copy-done.5
  69.2 1.1 fusion.23
  70.3 0.4 convolution_add_fusion.2
  70.7 24.7 %all-to-all-done = f32[2,1,2,256,128]{3,2,1,0,4:T(2,128)S(1)} async-done(((f32[2,1,2,256,128]{3,2,1,0,4:T(2,128)}), f32[2,1,2,256,128]{3,2,1,0,4:T(2,128)S(1)}, u32[]{:S(2)}, u32[]{:S(2)}) %all-to-all-start) | async-done | bytes 524320 | tf_op jit(solution)/shard_map/all_to_all | solution.py:117
  95.4 0.2 fusion.27
  95.6 0.2 squeeze.20
  95.8 0.2 squeeze.18
  96.0 0.8 copy-done.7
  96.7 1.4 multiply_subtract_fusion
  98.1 0.4 fusion.29
  98.5 0.4 fusion.28
  98.9 0.4 convolution_add_fusion.1
  99.3 0.4 convolution_subtract_fusion
  99.6 0.5 copy-done.9
  100.2 0.6 fusion.17
  100.8 0.3 copy-done.12
  101.1 1.2 fusion.7
  102.3 0.1 copy.37
  102.5 0.5 broadcast.6
  103.0 1.0 reduce
  104.0 23.9 %all_to_all.53 = bf16[128,2,128]{2,1,0:T(2,128)(2,1)S(1)} all-to-all(bf16[128,2,128]{2,1,0:T(2,128)(2,1)S(1)} %reshape.63), channel_id=1, replica_groups=mesh['tm'=128,'chan'=4] {'tm'}, dimensions={0} | all-to-all | bytes 131072 | tf_op jit(solution)/shard_map/all_to_all | solution.py:123
  128.0 0.7 stack.8
  128.7 3.5 %all-to-all-start.3 = ((bf16[4,256,128]{1,2,0:T(8,128)(2,1)}), bf16[4,256,128]{1,2,0:T(8,128)(2,1)S(1)}, u32[]{:S(2)}, u32[]{:S(2)}) async-start(bf16[4,256,128]{1,2,0:T(8,128)(2,1)} %stack.8), calls=%async_computation.3 | async-start | bytes 524288 | tf_op jit(solution)/shard_map/all_to_all | solution.py:125
  132.2 5.6 %all-to-all-done.3 = bf16[4,256,128]{1,2,0:T(8,128)(2,1)S(1)} async-done(((bf16[4,256,128]{1,2,0:T(8,128)(2,1)}), bf16[4,256,128]{1,2,0:T(8,128)(2,1)S(1)}, u32[]{:S(2)}, u32[]{:S(2)}) %all-to-all-start.3) | async-done | bytes 262176 | tf_op jit(solution)/shard_map/all_to_all | solution.py:125
  137.9 0.9 fusion.6
  (36 shorter events, 0.2 us)
Async XLA Ops:
  0.0 137.9 %copy-start = (bf16[512,512]{1,0:T(8,128)(2,1)S(1)}, bf16[512,512]{1,0:T(8,128)(2,1)}, u32[]{:S(2)}) copy-start(bf16[512,512]{1,0:T(8,128)(2,1)} %param.22) | copy-start | bytes 1572868
  0.0 1.2 copy-start.13
  1.2 10.3 %copy-start.15 = (f32[3,128]{1,0:T(4,128)S(1)}, f32[3,128]{1,0:T(4,128)}, u32[]{:S(2)}) copy-start(f32[3,128]{1,0:T(4,128)} %param.17) | copy-start | bytes 4612
  11.6 6.6 %copy-start.14 = (f32[3,3,128]{2,1,0:T(4,128)S(1)}, f32[3,3,128]{2,1,0:T(4,128)}, u32[]{:S(2)}) copy-start(f32[3,3,128]{2,1,0:T(4,128)} %param.18) | copy-start | bytes 13828
  11.9 9.6 %collective-permute-start = (bf16[2,3,128]{2,0,1:T(2,128)(2,1)S(1)}, bf16[2,3,128]{2,0,1:T(2,128)(2,1)S(1)}, u32[]{:S(2)}, u32[]{:S(2)}) collective-permute-start(bf16[2,3,128]{2,0,1:T(2,128)(2,1)S(1)} %slice.63), channel_id=1, source_target_pairs={{0,4},{4,8},{8,12},{12,16},{16,20},{20,24},{24,28},{28,32},{32,36}... | collective-permute-start | bytes 4616 | tf_op jit(solution)/shard_map/ppermute | solution.py:14
  21.5 0.7 copy-start.16
  22.4 19.1 %copy-start.10 = (f32[2,1,2,256,128]{4,3,2,1,0:T(8,128)S(1)}, f32[2,1,2,256,128]{4,3,2,1,0:T(8,128)}, u32[]{:S(2)}) copy-start(f32[2,1,2,256,128]{4,3,2,1,0:T(8,128)} %param.20) | copy-start | bytes 1572868
  23.3 34.2 %all-to-all-start.1 = ((bf16[2,1,256,128]{2,0,1,3:T(2,128)(2,1)}), bf16[2,1,256,128]{2,0,1,3:T(2,128)(2,1)S(1)}, u32[]{:S(2)}, u32[]{:S(2)}) async-start(bf16[2,1,256,128]{2,0,1,3:T(2,128)(2,1)} %copy.34), calls=%async_computation.1 | async-start | bytes 262144 | tf_op jit(solution)/shard_map/all_to_all | solution.py:114
  57.5 37.9 %all-to-all-start = ((f32[2,1,2,256,128]{3,2,1,0,4:T(2,128)}), f32[2,1,2,256,128]{3,2,1,0,4:T(2,128)S(1)}, u32[]{:S(2)}, u32[]{:S(2)}) async-start(f32[2,1,2,256,128]{3,2,1,0,4:T(2,128)} %copy.32), calls=%async_computation | async-start | bytes 1048576 | tf_op jit(solution)/shard_map/all_to_all | solution.py:117
  64.7 0.7 copy-start.18
  66.0 0.9 copy-start.11
  66.0 1.2 copy-start.8
  66.9 1.0 copy-start.3
  66.9 1.0 copy-start.6
  67.2 1.0 copy-start.2
  68.1 0.9 copy-start.1
  68.1 1.0 copy-start.5
  69.2 1.1 copy-start.4
  95.8 1.0 copy-start.7
  99.2 0.9 copy-start.9
  100.2 0.9 copy-start.12
  128.7 9.2 %all-to-all-start.3 = ((bf16[4,256,128]{1,2,0:T(8,128)(2,1)}), bf16[4,256,128]{1,2,0:T(8,128)(2,1)S(1)}, u32[]{:S(2)}, u32[]{:S(2)}) async-start(bf16[4,256,128]{1,2,0:T(8,128)(2,1)} %stack.8), calls=%async_computation.3 | async-start | bytes 524288 | tf_op jit(solution)/shard_map/all_to_all | solution.py:125
  132.2 5.6 %copy-start.17 = (f32[128]{0:T(128)S(1)}, f32[128]{0:T(128)}, u32[]{:S(2)}) copy-start(f32[128]{0:T(128)} %param.23) | copy-start | bytes 1540
